TPU v7x, 256 devices: a whole 4x4x8 slice. The times are simulated.
256 devices in a mesh: section: 16 (over y, x), dp: 16 (over z, core).
Axes of the slice: x: 4, y: 4, z: 8, core: 2. Of those that a mesh axis runs over, the one named last changes fastest.
Arguments:
- hidden: bfloat16 [16, 256, 8192], P('dp', 'section'), may hold values from -1500 to 1500
- head: bfloat16 [65536, 8192], P('section', 'dp'), may hold values from -0.0625 to 0.0625
- block_id: int32 [16, 16], P(None, 'section'), may hold values from 0 to 7
- block_live: int32 [16, 16], P(None, 'section'), may hold values from 0 to 1, as said below
- teacher: bfloat16 [16, 256, 8192], P('dp', None, 'section'), may hold values from -400 to 400
Outputs:
- grad_hidden: bfloat16 [16, 256, 8192], P('dp', 'section')
- grad_head: bfloat16 [65536, 8192], P('section', 'dp')
Inputs may be any that keep to these rules, and one draw needn't show every extreme that they name: `block_live`: every micro-batch has at least one live section.
All inputs are finite; a program needn't handle non-finite values.
Results may differ from a plain program's by a relative error of at most 0.0056.
Values may be sent and summed in bfloat16 or wider, within the bound.
No kernel may reach another device: no remote copies, remote signals or barrier semaphores. Data moves between devices by JAX's collectives and lax.ppermute only.
A program may use at most 128 MiB of HBM per device.

v0:
```python
import jax
import jax.numpy as jnp
from jax import lax
from jax.sharding import PartitionSpec as P

neg_fill = -1e30


def local(hidden, head, block_id, block_live, teacher):
    my_replica = lax.axis_index("dp")
    n_dp = lax.axis_size("dp")
    tok_local = hidden.shape[1]
    model_width = hidden.shape[2]
    block_rows = teacher.shape[2]
    col_width = head.shape[1]
    blocks = head.shape[0] // block_rows
    table = head.reshape(blocks, block_rows, col_width)
    block_ids = block_id[:, 0]
    live_flags = block_live[:, 0]
    n_mb = block_ids.shape[0]
    pieces = hidden.reshape(1, tok_local, n_dp, col_width)
    pieces = lax.all_to_all(pieces, "dp", split_axis=2, concat_axis=0, tiled=True)
    hid_w = lax.all_gather(pieces, "section", axis=1, tiled=True).reshape(n_mb, -1, col_width)
    picked = jnp.take(table, block_ids, axis=0)
    part = jnp.einsum("mtw,mrw->mtr", hid_w, picked, preferred_element_type=jnp.float32)
    logits = lax.psum_scatter(part, "dp", scatter_dimension=0, tiled=True)[0]
    own_live = lax.dynamic_index_in_dim(live_flags, my_replica, 0, keepdims=False) > 0
    teach = teacher[0].astype(jnp.float32)
    live_value = jnp.where(own_live, 1.0, 0.0).astype(jnp.float32)
    stud_local = jnp.where(own_live, jnp.max(logits, axis=1), neg_fill)
    teach_local = jnp.where(own_live, jnp.max(teach, axis=1), neg_fill)
    stud_top, teach_top = lax.pmax((stud_local, teach_local), "section")
    stud_part = jnp.where(own_live, jnp.sum(jnp.exp(logits - stud_top[:, None]), axis=1), 0.0)
    teach_part = jnp.where(own_live, jnp.sum(jnp.exp(teach - teach_top[:, None]), axis=1), 0.0)
    stud_total, teach_total, live_count = lax.psum((stud_part, teach_part, live_value), "section")
    student = jnp.where(own_live, jnp.exp(logits - stud_top[:, None]) / stud_total[:, None], 0.0)
    teach_prob = jnp.where(
        own_live, jnp.exp(teach - teach_top[:, None]) / teach_total[:, None], 0.0
    )
    logit_grad = (block_rows * live_count * (student - teach_prob)).astype(jnp.bfloat16)
    grads = lax.all_gather(logit_grad[None], "dp", axis=0, tiled=True)
    contrib = jnp.einsum("mtr,mtw->mrw", grads, hid_w, preferred_element_type=jnp.float32).astype(
        jnp.bfloat16
    )
    block_range = jnp.arange(blocks, dtype=jnp.int32)[None, :]
    selector = jnp.where(
        (live_flags[:, None] > 0) & (block_ids[:, None] == block_range), 1.0, 0.0
    ).astype(jnp.bfloat16)
    grad_head = jnp.einsum("mb,mrw->brw", selector, contrib, preferred_element_type=jnp.float32)
    grad_head = grad_head.astype(jnp.bfloat16).reshape(blocks * block_rows, col_width)
    ghid = jnp.einsum("mtr,mrw->mtw", grads, picked, preferred_element_type=jnp.float32)
    ghid = lax.psum_scatter(ghid, "section", scatter_dimension=1, tiled=True).astype(jnp.bfloat16)
    ghid = lax.all_to_all(ghid, "dp", split_axis=0, concat_axis=2, tiled=True)
    grad_hidden = ghid.reshape(1, tok_local, model_width)
    return (grad_hidden, grad_head)


def solution(mesh):
    placed = (
        P("dp", "section", None),
        P("section", "dp"),
        P(None, "section"),
        P(None, "section"),
        P("dp", None, "section"),
    )
    return jax.shard_map(
        local,
        mesh=mesh,
        in_specs=placed,
        out_specs=(P("dp", "section", None), P("section", "dp")),
        check_vma=False,
    )
```

profile of v0, /device:TPU:1, one launch (start us, length us, event | category | flops | bytes accessed | tf_op | source)
XLA Modules:
  0.0 412.9 jit_solution(15351352990721341709)
XLA Ops:
  7.2 1.0 copy.29
  8.2 21.6 %all_to_all.36 = bf16[1,16,16,512]{3,1,0,2:T(8,128)(2,1)} all-to-all(bf16[1,16,16,512]{3,1,0,2:T(8,128)(2,1)S(1)} %bitcast.54), channel_id=1, replica_groups=mesh['section'=16,'dp'=16] {'dp'}, dimensions={2} | all-to-all | bytes 524288 | tf_op jit(solution)/shard_map/all_to_all | solution.py:22
  29.8 0.0 reduce-scatter.3.cloned.1.call-start
  29.8 0.7 fusion.34
  30.5 7.0 %gather_fusion = bf16[16,512,512]{2,1,0:T(8,128)(2,1)} fusion(bf16[8,512,512]{2,1,0:T(8,128)(2,1)} %bitcast.50, s32[1024]{0:T(1024)S(1)} %pad_clamp_fusion), kind=kCustom, calls=%fused_computation | custom fusion | bytes 16777280 | tf_op jit(solution)/shard_map/jit(_take)/gather | solution.py:24
  37.5 45.8 %all-gather.6.cloned.1.call-done = bf16[16,1,256,1,512]{4,2,0,3,1:T(8,128)(2,1)} async-done(((bf16[16,1,16,1,512]{4,2,0,3,1:T(8,128)(2,1)}), bf16[16,1,256,1,512]{4,2,0,3,1:T(8,128)(2,1)}) %all-gather.6.cloned.1.call-update) | async-done | bytes 4194320 | tf_op jit(solution)/shard_map/all_gather | solution.py:23
  83.3 10.2 %fusion.6 = f32[16,256,512]{1,2,0:T(8,128)} fusion(bf16[16,1,256,1,512]{4,2,0,3,1:T(8,128)(2,1)} %all-gather.6.cloned.1.call-done, bf16[16,512,512]{2,1,0:T(8,128)(2,1)} %gather_fusion, pred[16]{0:T(512)(128)(4,1)S(1)} %and_bitcast_fusion), kind=kOutput, calls=%fused_computation.9 | convolution fusion | flops 2151677952 | bytes 20971536 | tf_op jit(solution)/shard_map/mtw,mrw->mtr/dot_general | solution.py:25
  93.5 0.9 copy-done
  94.4 0.1 copy.15
  94.6 0.1 reduce_max.24
  94.7 0.6 fusion.35
  95.9 0.6 convert_select_fusion
  96.6 64.4 %reduce-scatter.3.cloned.1.call-done = f32[1,256,512]{1,2,0:T(8,128)} async-done(((f32[16,256,512]{1,2,0:T(8,128)}), f32[1,256,512]{1,2,0:T(8,128)}) %reduce-scatter.3.cloned.1.call-update) | async-done | bytes 524304 | tf_op jit(solution)/shard_map/reduce_scatter | solution.py:26
  161.0 1.1 reduce_max.23
  162.1 0.6 broadcast_select_fusion.7
  162.8 33.3 %all-reduce.1 = (f32[256]{0:T(256)S(1)}, f32[256]{0:T(256)S(1)}) all-reduce(f32[256]{0:T(256)S(1)} %convert_select_fusion, f32[256]{0:T(256)S(1)} %broadcast_select_fusion.7), channel_id=1, replica_groups=mesh['section'=16,'dp'=16] {'section'}, use_global_device_ids=true, to_apply=%region_7.8 | all-reduce | flops 512 | bytes 4096 | tf_op jit(solution)/shard_map/pmax | solution.py:32
  196.1 0.1 fusion.19
  196.2 1.2 fusion.21
  197.4 0.6 broadcast_select_fusion.5
  198.0 29.2 %all-reduce = (f32[256]{0:T(256)S(1)}, f32[256]{0:T(256)S(1)}, f32[]{:T(128)}) all-reduce(f32[256]{0:T(256)S(1)} %get-tuple-element.7, f32[256]{0:T(256)S(1)} %get-tuple-element.8, f32[]{:T(128)S(6)} %select_n.58), channel_id=1, replica_groups=mesh['section'=16,'dp'=16] {'section'}, use_global_device_ids=true, to_apply=%region_9.10 | all-reduce | flops 513 | bytes 4104 | tf_op jit(solution)/shard_map/psum | solution.py:35
  227.9 1.9 fusion.22
  229.8 0.8 copy.16
  230.7 54.8 %all-gather.4.cloned.1.call-done = bf16[16,256,512]{2,1,0:T(8,128)(2,1)} async-done(((bf16[1,256,512]{2,1,0:T(8,128)(2,1)}), bf16[16,256,512]{2,1,0:T(8,128)(2,1)}) %all-gather.4.cloned.1.call-update) | async-done | bytes 4194320 | tf_op jit(solution)/shard_map/all_gather | solution.py:41
  285.5 10.3 %fusion.5 = f32[16,256,512]{2,1,0:T(8,128)} fusion(bf16[16,256,512]{2,1,0:T(8,128)(2,1)} %all-gather.4.cloned.1.call-done, bf16[16,512,512]{2,1,0:T(8,128)(2,1)} %gather_fusion, pred[16]{0:T(512)(128)(4,1)S(1)} %and_bitcast_fusion), kind=kOutput, calls=%fused_computation.8 | convolution fusion | flops 2151677952 | bytes 20971536 | tf_op jit(solution)/shard_map/mtr,mrw->mtw/dot_general | solution.py:51
  295.8 9.1 %convolution_convert_fusion = bf16[16,512,512]{2,1,0:T(8,128)(2,1)} fusion(bf16[16,256,512]{2,1,0:T(8,128)(2,1)} %all-gather.4.cloned.1.call-done, bf16[16,1,256,1,512]{4,2,0,3,1:T(8,128)(2,1)} %all-gather.6.cloned.1.call-done), kind=kOutput, calls=%fused_computation.4 | convolution fusion | flops 2151677952 | bytes 16777216 | tf_op jit(solution)/shard_map/mtr,mtw->mrw/dot_general | solution.py:42
  304.9 78.3 %reduce-scatter.5.cloned.1.call-done = f32[16,16,512]{2,1,0:T(8,128)} async-done(((f32[16,256,512]{2,1,0:T(8,128)}), f32[16,16,512]{2,1,0:T(8,128)}) %reduce-scatter.5.cloned.1.call-update) | async-done | bytes 524304 | tf_op jit(solution)/shard_map/reduce_scatter | solution.py:52
  383.2 1.8 convert_element_type.29
  385.0 9.0 %all-to-all-start.1 = ((bf16[16,16,512]{2,1,0:T(8,128)(2,1)}), bf16[16,16,512]{2,1,0:T(8,128)(2,1)S(1)}, u32[]{:S(2)}, u32[]{:S(2)}) async-start(bf16[16,16,512]{2,1,0:T(8,128)(2,1)} %convert_element_type.29), calls=%async_computation.3 | async-start | bytes 524288 | tf_op jit(solution)/shard_map/all_to_all | solution.py:53
  393.9 8.1 %fusion.9 = bf16[8,512,512]{2,0,1:T(8,128)(2,1)S(1)} fusion(bf16[16,512,512]{2,1,0:T(8,128)(2,1)} %convolution_convert_fusion, s32[16]{0:T(128)S(1)} %bitcast.57, pred[16]{0:T(512)(128)(4,1)S(1)} %compare_bitcast_fusion), kind=kOutput, calls=%fused_computation.10 | convolution fusion | flops 69206528 | bytes 12582992 | tf_op jit(solution)/shard_map/mb,mrw->brw/dot_general | solution.py:49
  402.0 3.5 copy.20
  405.5 0.1 all-to-all-done.1
  405.6 0.7 copy.23
  (15 shorter events, 0.2 us)
Async XLA Ops:
  7.2 76.1 %all-gather.6.cloned.1.call-start = ((), (), s32[]{:S(2)}) async-start(), calls=%async_computation.7 | async-start | bytes 4456448 | tf_op jit(solution)/shard_map/all_gather | solution.py:23
  29.8 131.2 %reduce-scatter.3.cloned.1.call-start = ((), (), s32[]{:S(2)}) async-start(), calls=%async_computation.4 | async-start | bytes 8912896 | tf_op jit(solution)/shard_map/reduce_scatter | solution.py:26
  30.5 7.0 %copy-start.1 = (s32[16,1]{0,1:T(1,128)S(1)}, s32[16,1]{0,1:T(1,128)}, u32[]{:S(2)}) copy-start(s32[16,1]{0,1:T(1,128)} %param.7) | copy-start | bytes 196
  93.5 0.9 copy-start
  93.5 1.2 copy-start.2
  93.5 192.0 %all-gather.4.cloned.1.call-start = ((), (), s32[]{:S(2)}) async-start(), calls=%async_computation.5 | async-start | bytes 4456448 | tf_op jit(solution)/shard_map/all_gather | solution.py:41
  230.7 152.5 %reduce-scatter.5.cloned.1.call-start = ((), (), s32[]{:S(2)}) async-start(), calls=%async_computation.6 | async-start | bytes 8912896 | tf_op jit(solution)/shard_map/reduce_scatter | solution.py:52
  385.0 20.7 %all-to-all-start.1 = ((bf16[16,16,512]{2,1,0:T(8,128)(2,1)}), bf16[16,16,512]{2,1,0:T(8,128)(2,1)S(1)}, u32[]{:S(2)}, u32[]{:S(2)}) async-start(bf16[16,16,512]{2,1,0:T(8,128)(2,1)} %convert_element_type.29), calls=%async_computation.3 | async-start | bytes 524288 | tf_op jit(solution)/shard_map/all_to_all | solution.py:53
Sparse Core Ops, SparseCore 0:
  29.9 53.3 all-gather.5
  93.6 67.3 reduce-scatter.2
  230.8 54.6 all-gather.3
  295.9 87.1 reduce-scatter.4
where the time goes:
time: 413 us
  waiting for transfers between devices  243 us (59%)
  blocking collectives  84.1 us (20%)
  matrix products  37.7 us (9%)
  between operations  15.1 us (4%)
  local copies, waits for them, and re-layouts  14 us (3%)
  other arithmetic  9.45 us (2%)
  starting transfers between devices  9.12 us (2%)
    reduce_scatter x1, waiting for transfers between devices, local(): lax.psum_scatter(ghid, 'section', scatter_dimension=1, tiled=True)  78.3 us
    reduce_scatter x1, waiting for transfers between devices, local(): logits = lax.psum_scatter(part, 'dp', scatter_dimension=0, tiled=True)[0]  64.4 us
    all_gather x1, waiting for transfers between devices, local(): grads = lax.all_gather(logit_grad[None], 'dp', axis=0, tiled=True)  54.8 us
    all_gather x1, waiting for transfers between devices, local(): lax.all_gather(pieces, 'section', axis=1, tiled=True)  45.8 us
    pmax x1, blocking collectives, local(): stud_top, teach_top = lax.pmax((stud_local, teach_local), 'section')  33.3 us
    psum x1, blocking collectives, local(): lax.psum((stud_part, teach_part, live_value), 'section')  29.2 us
    all_to_all x1, blocking collectives, local(): lax.all_to_all(pieces, 'dp', split_axis=2, concat_axis=0, tiled=True)  21.6 us
    dot_general x1, matrix products, local(): jnp.einsum('mtr,mrw->mtw', grads, picked, preferred_element_type=jnp.floa...  10.3 us
  transfers between devices with their start and end apart: 5, of which 5 were waited for; matrix products, arithmetic and copies ran while one was open for 7% of the time, Pallas kernels for 0%

commit v1 on v0

--- a/solution.py
+++ b/solution.py
@@ -20,7 +20,9 @@
     n_mb = block_ids.shape[0]
     pieces = hidden.reshape(1, tok_local, n_dp, col_width)
     pieces = lax.all_to_all(pieces, "dp", split_axis=2, concat_axis=0, tiled=True)
-    hid_w = lax.all_gather(pieces, "section", axis=1, tiled=True).reshape(n_mb, -1, col_width)
+    hid_w = jnp.concatenate(
+        lax.all_to_all(jnp.stack([pieces] * lax.axis_size("section")), "section", 0, 0), axis=1
+    ).reshape(n_mb, -1, col_width)
     picked = jnp.take(table, block_ids, axis=0)
     part = jnp.einsum("mtw,mrw->mtr", hid_w, picked, preferred_element_type=jnp.float32)
     logits = lax.psum_scatter(part, "dp", scatter_dimension=0, tiled=True)[0]

time: 413 us -> 431 us (1.044)
  local copies, waits for them, and re-layouts: 14 us -> 21.1 us
  starting transfers between devices: 9.12 us -> 15.8 us
  waiting for transfers between devices: 243 us -> 249 us
    all_to_all x0 -> x1, waiting for transfers between devices: none -> 58.4 us  [local(): lax.all_to_all(jnp.stack([pieces] * lax.axis_size('section')), 'section',...]
    all_gather x1 -> x0, waiting for transfers between devices: 45.8 us -> none  [local(): lax.all_gather(pieces, 'section', axis=1, tiled=True)]
    all_to_all x0 -> x1, starting transfers between devices: none -> 6.81 us  [local(): lax.all_to_all(jnp.stack([pieces] * lax.axis_size('section')), 'section',...]
    reduce_scatter x1, waiting for transfers between devices: 64.4 us -> 57.9 us  [local(): logits = lax.psum_scatter(part, 'dp', scatter_dimension=0, tiled=True)[0]]
where the time goes in v1:
time: 431 us
  waiting for transfers between devices  249 us (58%)
  blocking collectives  83.8 us (19%)
  matrix products  36.5 us (8%)
  local copies, waits for them, and re-layouts  21.1 us (5%)
  starting transfers between devices  15.8 us (4%)
  between operations  15.1 us (4%)
  other arithmetic  8.79 us (2%)
    reduce_scatter x1, waiting for transfers between devices, local(): lax.psum_scatter(ghid, 'section', scatter_dimension=1, tiled=True)  78.1 us
    all_to_all x1, waiting for transfers between devices, local(): lax.all_to_all(jnp.stack([pieces] * lax.axis_size('section')), 'section',...  58.4 us
    reduce_scatter x1, waiting for transfers between devices, local(): logits = lax.psum_scatter(part, 'dp', scatter_dimension=0, tiled=True)[0]  57.9 us
    all_gather x1, waiting for transfers between devices, local(): grads = lax.all_gather(logit_grad[None], 'dp', axis=0, tiled=True)  54.7 us
    pmax x1, blocking collectives, local(): stud_top, teach_top = lax.pmax((stud_local, teach_local), 'section')  33.2 us
    psum x1, blocking collectives, local(): lax.psum((stud_part, teach_part, live_value), 'section')  29.2 us
    all_to_all x1, blocking collectives, local(): lax.all_to_all(pieces, 'dp', split_axis=2, concat_axis=0, tiled=True)  21.5 us
    dot_general x1, matrix products, local(): jnp.einsum('mtr,mrw->mtw', grads, picked, preferred_element_type=jnp.floa...  10.3 us
  transfers between devices with their start and end apart: 5, of which 5 were waited for; matrix products, arithmetic and copies ran while one was open for 7% of the time, Pallas kernels for 0%

profile of v1, /device:TPU:1, one launch (start us, length us, event | category | flops | bytes accessed | tf_op | source)
XLA Modules:
  0.0 430.5 jit_solution(11105436985759427691)
XLA Ops:
  7.2 1.0 copy.38
  8.2 21.5 %all_to_all.38 = bf16[1,16,16,512]{3,1,0,2:T(8,128)(2,1)S(1)} all-to-all(bf16[1,16,16,512]{3,1,0,2:T(8,128)(2,1)S(1)} %bitcast.55), channel_id=1, replica_groups=mesh['section'=16,'dp'=16] {'dp'}, dimensions={2} | all-to-all | bytes 524288 | tf_op jit(solution)/shard_map/all_to_all | solution.py:22
  29.6 2.5 stack.5
  32.2 6.8 %all-to-all-start.1 = ((bf16[16,16,16,1,512]{4,2,1,3,0:T(8,128)(2,1)}), bf16[16,16,16,1,512]{4,2,1,3,0:T(8,128)(2,1)}, u32[]{:S(2)}, u32[]{:S(2)}) async-start(bf16[16,16,16,1,512]{4,2,1,3,0:T(8,128)(2,1)} %stack.5), calls=%async_computation.1 | async-start | bytes 8388608 | tf_op jit(solution)/shard_map/all_to_all | solution.py:24
  39.1 7.0 %gather_fusion = bf16[16,512,512]{2,1,0:T(8,128)(2,1)} fusion(bf16[8,512,512]{2,1,0:T(8,128)(2,1)} %bitcast.49, s32[1024]{0:T(1024)S(1)} %pad_clamp_fusion), kind=kCustom, calls=%fused_computation | custom fusion | bytes 16777280 | tf_op jit(solution)/shard_map/jit(_take)/gather | solution.py:26
  46.0 58.4 %all-to-all-done.1 = bf16[16,16,16,1,512]{4,2,1,3,0:T(8,128)(2,1)} async-done(((bf16[16,16,16,1,512]{4,2,1,3,0:T(8,128)(2,1)}), bf16[16,16,16,1,512]{4,2,1,3,0:T(8,128)(2,1)}, u32[]{:S(2)}, u32[]{:S(2)}) %all-to-all-start.1) | async-done | bytes 4194336 | tf_op jit(solution)/shard_map/all_to_all | solution.py:24
  104.4 2.6 copy.23
  107.1 2.0 copy-done
  109.1 9.0 %fusion.4 = f32[16,256,512]{1,2,0:T(8,128)} fusion(bf16[16,256,512]{2,1,0:T(8,128)(2,1)S(1)} %bitcast.50, bf16[16,512,512]{2,1,0:T(8,128)(2,1)} %gather_fusion, pred[16]{0:T(512)(128)(4,1)S(1)} %and_bitcast_fusion), kind=kOutput, calls=%fused_computation.7 | convolution fusion | flops 2151677952 | bytes 20971536 | tf_op jit(solution)/shard_map/mtw,mrw->mtr/dot_general | solution.py:27
  118.2 0.9 copy-done.1
  119.1 0.1 copy.24
  119.3 0.6 fusion.31
  120.6 0.6 convert_select_fusion
  121.2 57.9 %reduce-scatter.3.cloned.1.call-done = f32[1,256,512]{1,2,0:T(8,128)} async-done(((f32[16,256,512]{1,2,0:T(8,128)}), f32[1,256,512]{1,2,0:T(8,128)}) %reduce-scatter.3.cloned.1.call-update) | async-done | bytes 524304 | tf_op jit(solution)/shard_map/reduce_scatter | solution.py:28
  179.1 1.1 reduce_max.23
  180.3 0.6 broadcast_select_fusion.7
  180.9 33.2 %all-reduce.1 = (f32[256]{0:T(256)S(1)}, f32[256]{0:T(256)S(1)}) all-reduce(f32[256]{0:T(256)S(1)} %convert_select_fusion, f32[256]{0:T(256)S(1)} %broadcast_select_fusion.7), channel_id=1, replica_groups=mesh['section'=16,'dp'=16] {'section'}, use_global_device_ids=true, to_apply=%region_7.8 | all-reduce | flops 512 | bytes 4096 | tf_op jit(solution)/shard_map/pmax | solution.py:34
  214.2 1.2 fusion.17
  215.4 0.6 broadcast_select_fusion.5
  216.0 29.2 %all-reduce = (f32[256]{0:T(256)S(1)}, f32[256]{0:T(256)S(1)}, f32[]{:T(128)}) all-reduce(f32[256]{0:T(256)S(1)} %get-tuple-element.7, f32[256]{0:T(256)S(1)} %get-tuple-element.8, f32[]{:T(128)S(6)} %select_n.58), channel_id=1, replica_groups=mesh['section'=16,'dp'=16] {'section'}, use_global_device_ids=true, to_apply=%region_9.10 | all-reduce | flops 513 | bytes 4104 | tf_op jit(solution)/shard_map/psum | solution.py:37
  245.8 1.9 fusion.18
  247.7 0.8 copy.25
  248.6 54.7 %all-gather.2.cloned.1.call-done = bf16[16,256,512]{2,1,0:T(8,128)(2,1)} async-done(((bf16[1,256,512]{2,1,0:T(8,128)(2,1)}), bf16[16,256,512]{2,1,0:T(8,128)(2,1)}) %all-gather.2.cloned.1.call-update) | async-done | bytes 4194320 | tf_op jit(solution)/shard_map/all_gather | solution.py:43
  303.4 10.3 %fusion.2 = f32[16,256,512]{2,1,0:T(8,128)} fusion(bf16[16,256,512]{2,1,0:T(8,128)(2,1)} %all-gather.2.cloned.1.call-done, bf16[16,512,512]{2,1,0:T(8,128)(2,1)} %gather_fusion, pred[16]{0:T(512)(128)(4,1)S(1)} %and_bitcast_fusion), kind=kOutput, calls=%fused_computation.5 | convolution fusion | flops 2151677952 | bytes 20971536 | tf_op jit(solution)/shard_map/mtr,mrw->mtw/dot_general | solution.py:53
  313.7 9.1 %convolution_convert_fusion = bf16[16,512,512]{2,1,0:T(8,128)(2,1)} fusion(bf16[16,256,512]{2,1,0:T(8,128)(2,1)} %all-gather.2.cloned.1.call-done, bf16[16,256,512]{2,1,0:T(8,128)(2,1)} %bitcast.51), kind=kOutput, calls=%fused_computation.4 | convolution fusion | flops 2151677952 | bytes 16777216 | tf_op jit(solution)/shard_map/mtr,mtw->mrw/dot_general | solution.py:44
  322.8 78.1 %reduce-scatter.5.cloned.1.call-done = f32[16,16,512]{2,1,0:T(8,128)} async-done(((f32[16,256,512]{2,1,0:T(8,128)}), f32[16,16,512]{2,1,0:T(8,128)}) %reduce-scatter.5.cloned.1.call-update) | async-done | bytes 524304 | tf_op jit(solution)/shard_map/reduce_scatter | solution.py:54
  400.9 1.8 convert_element_type.29
  402.7 8.9 %all-to-all-start.2 = ((bf16[16,16,512]{2,1,0:T(8,128)(2,1)}), bf16[16,16,512]{2,1,0:T(8,128)(2,1)S(1)}, u32[]{:S(2)}, u32[]{:S(2)}) async-start(bf16[16,16,512]{2,1,0:T(8,128)(2,1)} %convert_element_type.29), calls=%async_computation.4 | async-start | bytes 524288 | tf_op jit(solution)/shard_map/all_to_all | solution.py:55
  411.6 8.1 %fusion.5 = bf16[8,512,512]{2,0,1:T(8,128)(2,1)S(1)} fusion(bf16[16,512,512]{2,1,0:T(8,128)(2,1)} %convolution_convert_fusion, s32[16]{0:T(128)S(1)} %bitcast.58, pred[16]{0:T(512)(128)(4,1)S(1)} %compare_bitcast_fusion), kind=kOutput, calls=%fused_computation.8 | convolution fusion | flops 69206528 | bytes 12582992 | tf_op jit(solution)/shard_map/mb,mrw->brw/dot_general | solution.py:51
  419.7 3.5 copy.29
  423.2 0.1 all-to-all-done.2
  423.3 0.7 copy.32
  (18 shorter events, 0.5 us)
Async XLA Ops:
  7.2 31.9 %copy-start.2 = (s32[16,1]{0,1:T(1,128)S(1)}, s32[16,1]{0,1:T(1,128)}, u32[]{:S(2)}) copy-start(s32[16,1]{0,1:T(1,128)} %param.7) | copy-start | bytes 196
  32.2 72.2 %all-to-all-start.1 = ((bf16[16,16,16,1,512]{4,2,1,3,0:T(8,128)(2,1)}), bf16[16,16,16,1,512]{4,2,1,3,0:T(8,128)(2,1)}, u32[]{:S(2)}, u32[]{:S(2)}) async-start(bf16[16,16,16,1,512]{4,2,1,3,0:T(8,128)(2,1)} %stack.5), calls=%async_computation.1 | async-start | bytes 8388608 | tf_op jit(solution)/shard_map/all_to_all | solution.py:24
  39.0 140.1 %reduce-scatter.3.cloned.1.call-start = ((), (), s32[]{:S(2)}) async-start(), calls=%async_computation.5 | async-start | bytes 8912896 | tf_op jit(solution)/shard_map/reduce_scatter | solution.py:28
  107.1 2.0 copy-start
  118.1 0.9 copy-start.1
  118.1 1.2 copy-start.3
  118.1 185.2 %all-gather.2.cloned.1.call-start = ((), (), s32[]{:S(2)}) async-start(), calls=%async_computation.6 | async-start | bytes 4456448 | tf_op jit(solution)/shard_map/all_gather | solution.py:43
  248.6 152.3 %reduce-scatter.5.cloned.1.call-start = ((), (), s32[]{:S(2)}) async-start(), calls=%async_computation.7 | async-start | bytes 8912896 | tf_op jit(solution)/shard_map/reduce_scatter | solution.py:54
  402.7 20.6 %all-to-all-start.2 = ((bf16[16,16,512]{2,1,0:T(8,128)(2,1)}), bf16[16,16,512]{2,1,0:T(8,128)(2,1)S(1)}, u32[]{:S(2)}, u32[]{:S(2)}) async-start(bf16[16,16,512]{2,1,0:T(8,128)(2,1)} %convert_element_type.29), calls=%async_computation.4 | async-start | bytes 524288 | tf_op jit(solution)/shard_map/all_to_all | solution.py:55
Sparse Core Ops, SparseCore 0:
  118.3 60.8 reduce-scatter.2
  248.7 54.5 all-gather.1
  313.8 87.0 reduce-scatter.4
